TPU v7x, 256 devices: a whole 4x4x8 slice. The times are simulated.
256 devices in a mesh: expert: 32 (over x, z), tensor: 8 (over y, core).
Axes of the slice: x: 4, y: 4, z: 8, core: 2. Of those that a mesh axis runs over, the one named last changes fastest.
Arguments:
- attn_vals: bfloat16 [2048, 4096], P('expert', 'tensor'), may hold values from -6 to 6
- residual: bfloat16 [2048, 4096], P('expert', 'tensor'), may hold values from -6 to 6
- out_weight: bfloat16 [4096, 4096], P('tensor'), may hold values from -0.09375 to 0.09375
- norm_gain: float32 [4096], P('tensor'), may hold values from 0.5 to 1.5
- router_weight: float32 [4096, 8], P('tensor'), may hold values from -0.09375 to 0.09375
- routes: int32 [2048, 2], P('expert'), may hold values from 0 to 7, all different within a row; in each aligned block of 64 rows (0 to 63, 64 to 127, ...) at most 32 rows name the same one
- w_gate: bfloat16 [32, 4096, 2048], P('expert', None, 'tensor'), may hold values from -0.09375 to 0.09375
- w_up: bfloat16 [32, 4096, 2048], P('expert', None, 'tensor'), may hold values from -0.09375 to 0.09375
- w_down: bfloat16 [32, 2048, 4096], P('expert', 'tensor'), may hold values from -0.0625 to 0.0625
- slab_of: int32 [32], replicated, may hold values from 0 to 31, each once
- final_gain: float32 [4096], P('tensor'), may hold values from 0.5 to 1.5
- row_order: int32 [2048], replicated, may hold values from 0 to 2047, each once
Outputs:
- stream_out: bfloat16 [2048, 4096], P('expert', 'tensor')
- normed_out: bfloat16 [2048, 4096], P('expert', 'tensor')
Inputs may be any that keep to these rules, and one draw needn't show every extreme that they name: `routes`: the two experts of a row differ. In each aligned block of 64 rows (the rows of one device) no expert is named by more than 32 rows, and some block names one expert exactly 32 times. `slab_of`: A permutation. `row_order`: A permutation.
All inputs are finite; a program needn't handle non-finite values.
Results may differ from a plain program's by a relative error of at most 0.017.
Values may be sent and summed in bfloat16 or wider, within the bound.
No kernel may reach another device: no remote copies, remote signals or barrier semaphores. Data moves between devices by JAX's collectives and lax.ppermute only.
A program may use at most 128 MiB of HBM per device.

v0:
```python
import jax
import jax.numpy as jnp
from jax import lax
from jax.sharding import PartitionSpec as P

D = 4096
MOST = 32
EPS = 1e-05


def finish_slots(gate_val, up_val, down_weight):
    active = (jax.nn.silu(gate_val) * up_val).astype(jnp.bfloat16)
    partial_out = jnp.einsum("gmf,fd->gmd", active, down_weight, preferred_element_type=jnp.float32)
    summed = lax.psum_scatter(
        partial_out.astype(jnp.bfloat16), "tensor", scatter_dimension=2, tiled=True
    )
    return lax.all_to_all(summed, "expert", split_axis=0, concat_axis=0, tiled=True)


def final_norm(stream, final_gain):
    stream_f = stream.astype(jnp.float32)
    square_total = lax.psum(jnp.sum(stream_f * stream_f, axis=1), "tensor")
    factor = lax.rsqrt(square_total / D + EPS)
    return (stream_f * factor[:, None] * final_gain).astype(jnp.bfloat16)


def on_device(
    attn_vals,
    residual,
    out_weight,
    norm_gain,
    router_weight,
    routes,
    w_gate,
    w_up,
    w_down,
    slab_of,
    final_gain,
    row_order,
):
    groups = lax.axis_size("expert")
    row_count = attn_vals.shape[0]
    expert_count = router_weight.shape[1]
    slab_count = groups // expert_count
    partial_proj = jnp.dot(attn_vals, out_weight, preferred_element_type=jnp.float32)
    project = lax.psum_scatter(
        partial_proj.astype(jnp.bfloat16), "tensor", scatter_dimension=1, tiled=True
    ).astype(jnp.float32)
    stream_in = (residual.astype(jnp.float32) + project).astype(jnp.bfloat16)
    hidden_f = stream_in.astype(jnp.float32)
    scaled = hidden_f * norm_gain
    square_sum, logit_part = lax.psum(
        (
            jnp.sum(hidden_f * hidden_f, axis=1),
            jnp.dot(scaled, router_weight, precision=lax.Precision.HIGHEST),
        ),
        "tensor",
    )
    inverse_rms = lax.rsqrt(square_sum / D + EPS)
    normed_in = (scaled * inverse_rms[:, None]).astype(jnp.bfloat16)
    logits = logit_part * inverse_rms[:, None]
    expert_ids = jnp.arange(expert_count, dtype=jnp.int32)
    route_hot = (routes[:, :, None] == expert_ids[None, None, :]).astype(jnp.int32)
    chosen = jnp.sum(route_hot.astype(jnp.float32) * logits[:, None, :], axis=2)
    leading = jax.nn.sigmoid(chosen[:, 0] - chosen[:, 1])
    mixing = jnp.stack([leading, 1.0 - leading], axis=1)
    route_hits = jnp.sum(route_hot, axis=1)
    before_count = jnp.cumsum(route_hits, axis=0) - route_hits
    slot_ids = jnp.sum(route_hot * before_count[:, None, :], axis=2)
    slot_hot = (slot_ids[:, :, None] == jnp.arange(MOST, dtype=jnp.int32)[None, None, :]).astype(
        jnp.float32
    )
    placing = jnp.einsum("rke,rks->esr", route_hot.astype(jnp.float32), slot_hot).astype(
        jnp.bfloat16
    )
    target_expert = slab_of // slab_count
    send_map = jnp.take(placing, target_expert, axis=0)
    outgoing = jnp.einsum(
        "gsr,rd->gsd", send_map, normed_in, preferred_element_type=jnp.float32
    ).astype(jnp.bfloat16)
    arrived_part = lax.all_to_all(outgoing, "expert", split_axis=0, concat_axis=0, tiled=True)
    arrived = lax.all_gather(arrived_part, "tensor", axis=2, tiled=True)
    gate_val = jnp.einsum("gmd,df->gmf", arrived, w_gate[0], preferred_element_type=jnp.float32)
    up_val = jnp.einsum("gmd,df->gmf", arrived, w_up[0], preferred_element_type=jnp.float32)
    returned = finish_slots(gate_val, up_val, w_down[0])
    group_ids = jnp.arange(groups, dtype=jnp.int32)
    holder_hot = (slab_of[None, :] == group_ids[:, None]).astype(jnp.int32)
    holders = jnp.sum(holder_hot * group_ids[None, :], axis=1).reshape(expert_count, slab_count)
    row_holders = jnp.take(holders, routes, axis=0)
    flat_index = row_holders * MOST + slot_ids[:, :, None]
    flat_back = returned.reshape(groups * MOST, returned.shape[2])
    fetched = jnp.take(flat_back, flat_index.reshape(-1), axis=0).reshape(
        row_count, 2, slab_count, returned.shape[2]
    )
    expert_out = jnp.sum(fetched.astype(jnp.float32), axis=2)
    blended = jnp.sum(mixing[:, :, None] * expert_out, axis=1)
    stream = (hidden_f + blended).astype(jnp.bfloat16)
    positions = lax.axis_index("expert") * row_count + jnp.arange(row_count, dtype=jnp.int32)
    matches = (row_order[None, :] == positions[:, None]).astype(jnp.int32)
    source = jnp.sum(matches * jnp.arange(row_order.shape[0], dtype=jnp.int32)[None, :], axis=1)
    all_stream = lax.all_gather(stream, "expert", axis=0, tiled=True)
    ordered = jnp.take(all_stream, source, axis=0)
    return (ordered, final_norm(ordered, final_gain))


def solution(mesh):
    return jax.shard_map(
        on_device,
        mesh=mesh,
        in_specs=(
            P("expert", "tensor"),
            P("expert", "tensor"),
            P("tensor", None),
            P("tensor"),
            P("tensor", None),
            P("expert", None),
            P("expert", None, "tensor"),
            P("expert", None, "tensor"),
            P("expert", "tensor", None),
            P(),
            P("tensor"),
            P(),
        ),
        out_specs=(P("expert", "tensor"), P("expert", "tensor")),
        check_vma=False,
    )
```

profile of v0, /device:TPU:1, one launch (start us, length us, event | category | flops | bytes accessed | tf_op | source)
XLA Modules:
  0.0 367.0 jit_solution(5263027604369193061)
XLA Ops:
  7.2 4.0 %convolution_convert_fusion.1 = bf16[64,4096]{1,0:T(8,128)(2,1)} fusion(bf16[64,512]{1,0:T(8,128)(2,1)} %param.12, bf16[512,4096]{1,0:T(8,128)(2,1)} %param.14), kind=kOutput, calls=%fused_computation.5 | convolution fusion | flops 268697600 | bytes 4784128 | tf_op jit(solution)/shard_map/dot_general | solution.py:45
  11.3 0.1 copy.71
  11.4 0.2 convert_reduce_fusion.1
  11.6 0.1 reduce_window_sum.11
  11.7 1.2 select_reduce_fusion.1
  12.9 0.4 fusion.13
  13.4 0.1 copy.80
  13.6 0.6 gather_fusion.1
  14.2 32.7 %reduce-scatter.3.cloned.1.call-done = bf16[64,512]{1,0:T(8,128)(2,1)} async-done(((bf16[64,4096]{1,0:T(8,128)(2,1)}), bf16[64,512]{1,0:T(8,128)(2,1)}) %reduce-scatter.3.cloned.1.call-update) | async-done | bytes 65552 | tf_op jit(solution)/shard_map/reduce_scatter | solution.py:46
  46.8 1.0 fusion.28
  47.8 0.2 fusion.23
  48.0 14.9 %all-reduce = (f32[64]{0:T(128)S(1)}, f32[64,8]{0,1:T(8,128)S(1)}) all-reduce(f32[64]{0:T(128)S(1)} %get-tuple-element.10, f32[64,8]{0,1:T(8,128)S(1)} %fusion.23), channel_id=1, replica_groups=mesh['expert'=32,'tensor'=8] {'tensor'}, use_global_device_ids=true, to_apply=%region_4.0 | all-reduce | flops 576 | bytes 4608 | tf_op jit(solution)/shard_map/psum | solution.py:52
  62.9 0.5 convolution_convert_fusion.2
  63.4 34.6 %all_to_all.10 = bf16[32,32,512]{2,1,0:T(8,128)(2,1)} all-to-all(bf16[32,32,512]{2,1,0:T(8,128)(2,1)S(1)} %convolution_convert_fusion.2), channel_id=1, replica_groups=mesh['expert'=32,'tensor'=8] {'expert'}, dimensions={0} | all-to-all | bytes 2097152 | tf_op jit(solution)/shard_map/all_to_all | solution.py:81
  98.1 50.6 %all-gather.3.cloned.1.call-done = bf16[32,32,4096]{2,1,0:T(8,128)(2,1)} async-done(((bf16[32,32,512]{2,1,0:T(8,128)(2,1)}), bf16[32,32,4096]{2,1,0:T(8,128)(2,1)}) %all-gather.3.cloned.1.call-update) | async-done | bytes 8388624 | tf_op jit(solution)/shard_map/all_gather | solution.py:82
  148.7 6.3 %fusion.3 = f32[32,32,256]{2,1,0:T(8,128)S(1)} fusion(bf16[32,32,4096]{2,1,0:T(8,128)(2,1)} %all-gather.3.cloned.1.call-done, bf16[1,4096,256]{2,1,0:T(8,128)(2,1)} %param.18), kind=kOutput, calls=%fused_computation.9 | convolution fusion | flops 2147483648 | bytes 11534336 | tf_op jit(solution)/shard_map/gmd,df->gmf/dot_general | solution.py:83
  155.0 16.8 %convolution_convert_fusion = bf16[32,32,4096]{2,1,0:T(8,128)(2,1)} fusion(bf16[1,256,4096]{2,1,0:T(8,128)(2,1)S(1)} %copy-done, bf16[32,32,4096]{2,1,0:T(8,128)(2,1)} %all-gather.3.cloned.1.call-done, bf16[1,4096,256]{2,1,0:T(8,128)(2,1)} %param.19, f32[32,32,256]{2,1,0:T(8,128)S(1)} %fusion.3), kind=kOutput, calls=%fused_computation.4 | convolution fusion | flops 4300734464 | bytes 22020096 | tf_op jit(solution)/shard_map/gmf,fd->gmd/dot_general | solution.py:13
  171.8 54.4 %reduce-scatter.5.cloned.1.call-done = bf16[32,32,512]{2,1,0:T(8,128)(2,1)} async-done(((bf16[32,32,4096]{2,1,0:T(8,128)(2,1)}), bf16[32,32,512]{2,1,0:T(8,128)(2,1)}) %reduce-scatter.5.cloned.1.call-update) | async-done | bytes 1048592 | tf_op jit(solution)/shard_map/reduce_scatter | solution.py:14
  226.2 9.5 %all-to-all-start.1 = ((bf16[32,32,512]{2,1,0:T(8,128)(2,1)}), bf16[32,32,512]{2,1,0:T(8,128)(2,1)S(1)}, u32[]{:S(2)}, u32[]{:S(2)}) async-start(bf16[32,32,512]{2,1,0:T(8,128)(2,1)} %reduce-scatter.5.cloned.1.call-done), calls=%async_computation.3 | async-start | bytes 2097152 | tf_op jit(solution)/shard_map/all_to_all | solution.py:17
  235.8 0.2 all-gather.5.cloned.1.call-start
  236.0 0.1 copy.78
  236.1 0.1 copy.76
  236.2 0.1 reshape.129
  236.3 0.1 select_reduce_fusion.2
  236.5 0.1 reshape.125
  236.6 0.6 gather_fusion
  237.2 0.1 copy.77
  237.3 0.1 copy.81
  237.4 0.1 add.139
  237.6 0.1 copy.79
  237.8 0.1 copy.72
  237.9 0.2 fusion.33
  238.1 0.1 fusion.45
  238.2 0.1 copy.84
  238.2 0.1 copy.85
  238.4 0.1 copy.75
  238.4 22.5 %all-to-all-done.1 = bf16[32,32,512]{2,1,0:T(8,128)(2,1)S(1)} async-done(((bf16[32,32,512]{2,1,0:T(8,128)(2,1)}), bf16[32,32,512]{2,1,0:T(8,128)(2,1)S(1)}, u32[]{:S(2)}, u32[]{:S(2)}) %all-to-all-start.1) | async-done | bytes 1048608 | tf_op jit(solution)/shard_map/all_to_all | solution.py:17
  261.0 2.6 gather_fusion.2
  263.6 1.2 gather.21
  264.8 0.9 convert_reduce_fusion
  265.7 0.4 multiply_reduce_fusion
  266.1 0.6 fusion.29
  266.8 0.2 select_reduce_fusion
  267.1 72.8 %all-gather.5.cloned.1.call-done = bf16[2048,512]{1,0:T(8,128)(2,1)} async-done(((bf16[64,512]{1,0:T(8,128)(2,1)}), bf16[2048,512]{1,0:T(8,128)(2,1)}) %all-gather.5.cloned.1.call-update) | async-done | bytes 2097168 | tf_op jit(solution)/shard_map/all_gather | solution.py:101
  339.9 2.6 gather_fusion.3
  342.5 0.2 fusion.25
  342.7 17.1 %psum.23 = f32[64]{0:T(128)S(1)} all-reduce(f32[64]{0:T(128)S(1)} %get-tuple-element.4), channel_id=1, replica_groups=mesh['expert'=32,'tensor'=8] {'tensor'}, use_global_device_ids=true, to_apply=%region_14.15 | all-reduce | flops 64 | bytes 512 | tf_op jit(solution)/shard_map/psum | solution.py:22
  359.7 0.7 fusion.27
  (43 shorter events, 0.4 us)
Async XLA Ops:
  7.2 147.8 %copy-start = (bf16[1,256,4096]{2,1,0:T(8,128)(2,1)S(1)}, bf16[1,256,4096]{2,1,0:T(8,128)(2,1)}, u32[]{:S(2)}) copy-start(bf16[1,256,4096]{2,1,0:T(8,128)(2,1)} %param.20) | copy-start | bytes 6291460
  7.2 4.1 %copy-start.6 = (s32[64,2]{0,1:T(2,128)S(1)}, s32[64,2]{0,1:T(2,128)}, u32[]{:S(2)}) copy-start(s32[64,2]{0,1:T(2,128)} %param.17) | copy-start | bytes 1540
  7.2 39.6 %reduce-scatter.3.cloned.1.call-start = ((), (), s32[]{:S(2)}) async-start(), calls=%async_computation.4 | async-start | bytes 589824 | tf_op jit(solution)/shard_map/reduce_scatter | solution.py:46
  11.2 2.3 copy-start.8
  11.2 35.6 %copy-start.2 = (bf16[64,512]{1,0:T(8,128)(2,1)S(1)}, bf16[64,512]{1,0:T(8,128)(2,1)}, u32[]{:S(2)}) copy-start(bf16[64,512]{1,0:T(8,128)(2,1)} %param.13) | copy-start | bytes 196612
  11.2 36.6 %copy-start.3 = (f32[512,8]{0,1:T(8,128)S(1)}, f32[512,8]{0,1:T(8,128)}, u32[]{:S(2)}) copy-start(f32[512,8]{0,1:T(8,128)} %param.16) | copy-start | bytes 49156
  11.2 36.6 %copy-start.4 = (f32[512]{0:T(512)S(1)}, f32[512]{0:T(512)}, u32[]{:S(2)}) copy-start(f32[512]{0:T(512)} %param.15) | copy-start | bytes 6148
  11.3 137.4 %all-gather.3.cloned.1.call-start = ((), (), s32[]{:S(2)}) async-start(), calls=%async_computation.5 | async-start | bytes 9437184 | tf_op jit(solution)/shard_map/all_gather | solution.py:82
  98.0 128.2 %reduce-scatter.5.cloned.1.call-start = ((), (), s32[]{:S(2)}) async-start(), calls=%async_computation.6 | async-start | bytes 9437184 | tf_op jit(solution)/shard_map/reduce_scatter | solution.py:14
  226.2 34.7 %all-to-all-start.1 = ((bf16[32,32,512]{2,1,0:T(8,128)(2,1)}), bf16[32,32,512]{2,1,0:T(8,128)(2,1)S(1)}, u32[]{:S(2)}, u32[]{:S(2)}) async-start(bf16[32,32,512]{2,1,0:T(8,128)(2,1)} %reduce-scatter.5.cloned.1.call-done), calls=%async_computation.3 | async-start | bytes 2097152 | tf_op jit(solution)/shard_map/all_to_all | solution.py:17
  235.8 104.1 %all-gather.5.cloned.1.call-start = ((), (), s32[]{:S(2)}) async-start(), calls=%async_computation.7 | async-start | bytes 2162688 | tf_op jit(solution)/shard_map/all_gather | solution.py:101
  263.6 3.2 copy-start.5
  263.6 96.2 %copy-start.7 = (f32[512]{0:T(512)S(1)}, f32[512]{0:T(512)}, u32[]{:S(2)}) copy-start(f32[512]{0:T(512)} %param.22) | copy-start | bytes 6148
  342.6 17.8 %copy-start.1 = (bf16[64,512]{1,0:T(8,128)(2,1)}, bf16[64,512]{1,0:T(8,128)(2,1)S(1)}, u32[]{:S(2)}) copy-start(bf16[64,512]{1,0:T(8,128)(2,1)S(1)} %get-tuple-element.5) | copy-start | bytes 196612
Sparse Core Ops, SparseCore 0:
  11.4 35.4 reduce-scatter.2
  98.1 50.5 all-gather.2
  172.0 54.2 reduce-scatter.4
  266.9 72.9 all-gather.4
where the time goes:
time: 367 us
  waiting for transfers between devices  233 us (63%)
  blocking collectives  66.5 us (18%)
  matrix products  28.2 us (8%)
  between operations  14.1 us (4%)
  starting transfers between devices  9.88 us (3%)
  local copies, waits for them, and re-layouts  9.17 us (2%)
  other arithmetic  6.03 us (2%)
    all_gather x1, waiting for transfers between devices, on_device(): all_stream = lax.all_gather(stream, 'expert', axis=0, tiled=True)  72.8 us
    reduce_scatter x1, waiting for transfers between devices, finish_slots(): lax.psum_scatter(partial_out.astype(jnp.bfloat16), 'tensor', scatter_dime...  54.4 us
    all_gather x1, waiting for transfers between devices, on_device(): arrived = lax.all_gather(arrived_part, 'tensor', axis=2, tiled=True)  50.6 us
    all_to_all x1, blocking collectives, on_device(): lax.all_to_all(outgoing, 'expert', split_axis=0, concat_axis=0, tiled=True)  34.6 us
    reduce_scatter x1, waiting for transfers between devices, on_device(): lax.psum_scatter(partial_proj.astype(jnp.bfloat16), 'tensor', scatter_dim...  32.7 us
    all_to_all x1, waiting for transfers between devices, finish_slots(): lax.all_to_all(summed, 'expert', split_axis=0, concat_axis=0, tiled=True)  22.5 us
    psum x1, blocking collectives, final_norm(): square_total = lax.psum(jnp.sum(stream_f * stream_f, axis=1), 'tensor')  17.1 us
    dot_general x1, matrix products, finish_slots(): jnp.einsum('gmf,fd->gmd', active, down_weight, preferred_element_type=jnp...  16.8 us
  transfers between devices with their start and end apart: 5, of which 5 were waited for; matrix products, arithmetic and copies ran while one was open for 1% of the time, Pallas kernels for 0%

commit v1 on v0

--- a/solution.py
+++ b/solution.py
@@ -19,7 +19,7 @@
 
 def final_norm(stream, final_gain):
     stream_f = stream.astype(jnp.float32)
-    square_total = lax.psum(jnp.sum(stream_f * stream_f, axis=1), "tensor")
+    square_total = jnp.sum(lax.all_gather(jnp.sum(stream_f * stream_f, axis=1), "tensor"), axis=0)
     factor = lax.rsqrt(square_total / D + EPS)
     return (stream_f * factor[:, None] * final_gain).astype(jnp.bfloat16)
 

time: 367 us -> 368 us (level)
    psum x1 -> x0, blocking collectives: 17.1 us -> none  [final_norm(): square_total = lax.psum(jnp.sum(stream_f * stream_f, axis=1), 'tensor')]
    unnamed x0 -> x1, blocking collectives: none -> 17.1 us
  transfers between devices with their start and end apart: 5 -> 5, of which waited for: 5 -> 5; matrix products, arithmetic and copies ran while one was open for 1% -> 2% of each run, Pallas kernels for 0% -> 0%
where the time goes in v1:
time: 368 us; the launch traced here: 367 us
  waiting for transfers between devices  232 us (63%)
  blocking collectives  66.5 us (18%)
  matrix products  28.2 us (8%)
  between operations  14.7 us (4%)
  local copies, waits for them, and re-layouts  10.1 us (3%)
  starting transfers between devices  9.88 us (3%)
  other arithmetic  6.05 us (2%)
    all_gather x1, waiting for transfers between devices, on_device(): all_stream = lax.all_gather(stream, 'expert', axis=0, tiled=True)  71.6 us
    reduce_scatter x1, waiting for transfers between devices, finish_slots(): lax.psum_scatter(partial_out.astype(jnp.bfloat16), 'tensor', scatter_dime...  54.4 us
    all_gather x1, waiting for transfers between devices, on_device(): arrived = lax.all_gather(arrived_part, 'tensor', axis=2, tiled=True)  50.6 us
    all_to_all x1, blocking collectives, on_device(): lax.all_to_all(outgoing, 'expert', split_axis=0, concat_axis=0, tiled=True)  34.6 us
    reduce_scatter x1, waiting for transfers between devices, on_device(): lax.psum_scatter(partial_proj.astype(jnp.bfloat16), 'tensor', scatter_dim...  32.7 us
    all_to_all x1, waiting for transfers between devices, finish_slots(): lax.all_to_all(summed, 'expert', split_axis=0, concat_axis=0, tiled=True)  22.5 us
    unnamed x1, blocking collectives  17.1 us
    dot_general x1, matrix products, finish_slots(): jnp.einsum('gmf,fd->gmd', active, down_weight, preferred_element_type=jnp...  16.8 us
  transfers between devices with their start and end apart: 5, of which 5 were waited for; matrix products, arithmetic and copies ran while one was open for 2% of the time, Pallas kernels for 0%

profile of v1, /device:TPU:1, one launch (start us, length us, event | category | flops | bytes accessed | tf_op | source)
XLA Modules:
  0.0 367.4 jit_solution(320725291776440441)
XLA Ops:
  7.2 4.0 %convolution_convert_fusion.1 = bf16[64,4096]{1,0:T(8,128)(2,1)} fusion(bf16[64,512]{1,0:T(8,128)(2,1)} %param.12, bf16[512,4096]{1,0:T(8,128)(2,1)} %param.14), kind=kOutput, calls=%fused_computation.5 | convolution fusion | flops 268697600 | bytes 4784128 | tf_op jit(solution)/shard_map/dot_general | solution.py:45
  11.3 0.1 copy.71
  11.4 0.2 convert_reduce_fusion.1
  11.6 0.1 reduce_window_sum.11
  11.7 1.2 select_reduce_fusion.1
  12.9 0.4 fusion.13
  13.4 0.1 copy.80
  13.6 0.6 gather_fusion.1
  14.2 32.7 %reduce-scatter.3.cloned.1.call-done = bf16[64,512]{1,0:T(8,128)(2,1)} async-done(((bf16[64,4096]{1,0:T(8,128)(2,1)}), bf16[64,512]{1,0:T(8,128)(2,1)}) %reduce-scatter.3.cloned.1.call-update) | async-done | bytes 65552 | tf_op jit(solution)/shard_map/reduce_scatter | solution.py:46
  46.8 1.0 fusion.28
  47.8 0.2 fusion.23
  48.0 14.9 %all-reduce.1 = (f32[64]{0:T(128)S(1)}, f32[64,8]{0,1:T(8,128)S(1)}) all-reduce(f32[64]{0:T(128)S(1)} %get-tuple-element.10, f32[64,8]{0,1:T(8,128)S(1)} %fusion.23), channel_id=1, replica_groups=mesh['expert'=32,'tensor'=8] {'tensor'}, use_global_device_ids=true, to_apply=%region_4.0 | all-reduce | flops 576 | bytes 4608 | tf_op jit(solution)/shard_map/psum | solution.py:52
  62.9 0.5 convolution_convert_fusion.2
  63.4 34.6 %all_to_all.10 = bf16[32,32,512]{2,1,0:T(8,128)(2,1)} all-to-all(bf16[32,32,512]{2,1,0:T(8,128)(2,1)S(1)} %convolution_convert_fusion.2), channel_id=1, replica_groups=mesh['expert'=32,'tensor'=8] {'expert'}, dimensions={0} | all-to-all | bytes 2097152 | tf_op jit(solution)/shard_map/all_to_all | solution.py:81
  98.1 50.6 %all-gather.4.cloned.1.call-done = bf16[32,32,4096]{2,1,0:T(8,128)(2,1)} async-done(((bf16[32,32,512]{2,1,0:T(8,128)(2,1)}), bf16[32,32,4096]{2,1,0:T(8,128)(2,1)}) %all-gather.4.cloned.1.call-update) | async-done | bytes 8388624 | tf_op jit(solution)/shard_map/all_gather | solution.py:82
  148.7 6.3 %fusion.3 = f32[32,32,256]{2,1,0:T(8,128)S(1)} fusion(bf16[32,32,4096]{2,1,0:T(8,128)(2,1)} %all-gather.4.cloned.1.call-done, bf16[1,4096,256]{2,1,0:T(8,128)(2,1)} %param.18), kind=kOutput, calls=%fused_computation.9 | convolution fusion | flops 2147483648 | bytes 11534336 | tf_op jit(solution)/shard_map/gmd,df->gmf/dot_general | solution.py:83
  155.0 16.8 %convolution_convert_fusion = bf16[32,32,4096]{2,1,0:T(8,128)(2,1)} fusion(bf16[1,256,4096]{2,1,0:T(8,128)(2,1)S(1)} %copy-done, bf16[32,32,4096]{2,1,0:T(8,128)(2,1)} %all-gather.4.cloned.1.call-done, bf16[1,4096,256]{2,1,0:T(8,128)(2,1)} %param.19, f32[32,32,256]{2,1,0:T(8,128)S(1)} %fusion.3), kind=kOutput, calls=%fused_computation.4 | convolution fusion | flops 4300734464 | bytes 22020096 | tf_op jit(solution)/shard_map/gmf,fd->gmd/dot_general | solution.py:13
  171.8 54.4 %reduce-scatter.5.cloned.1.call-done = bf16[32,32,512]{2,1,0:T(8,128)(2,1)} async-done(((bf16[32,32,4096]{2,1,0:T(8,128)(2,1)}), bf16[32,32,512]{2,1,0:T(8,128)(2,1)}) %reduce-scatter.5.cloned.1.call-update) | async-done | bytes 1048592 | tf_op jit(solution)/shard_map/reduce_scatter | solution.py:14
  226.2 9.5 %all-to-all-start.1 = ((bf16[32,32,512]{2,1,0:T(8,128)(2,1)}), bf16[32,32,512]{2,1,0:T(8,128)(2,1)S(1)}, u32[]{:S(2)}, u32[]{:S(2)}) async-start(bf16[32,32,512]{2,1,0:T(8,128)(2,1)} %reduce-scatter.5.cloned.1.call-done), calls=%async_computation.3 | async-start | bytes 2097152 | tf_op jit(solution)/shard_map/all_to_all | solution.py:17
  235.8 0.2 all-gather.6.cloned.1.call-start
  236.1 0.1 copy.76
  236.2 0.1 reshape.133
  236.3 0.1 select_reduce_fusion.2
  236.5 0.1 reshape.129
  236.6 0.6 gather_fusion
  237.2 0.1 copy.77
  237.3 0.1 copy.81
  237.4 0.1 add.141
  237.6 0.1 copy.79
  237.8 0.1 copy.72
  237.9 0.2 fusion.33
  238.1 0.1 fusion.45
  238.4 0.1 copy.75
  238.4 22.5 %all-to-all-done.1 = bf16[32,32,512]{2,1,0:T(8,128)(2,1)S(1)} async-done(((bf16[32,32,512]{2,1,0:T(8,128)(2,1)}), bf16[32,32,512]{2,1,0:T(8,128)(2,1)S(1)}, u32[]{:S(2)}, u32[]{:S(2)}) %all-to-all-start.1) | async-done | bytes 1048608 | tf_op jit(solution)/shard_map/all_to_all | solution.py:17
  261.0 2.6 gather_fusion.2
  263.6 1.2 gather.21
  264.8 0.9 convert_reduce_fusion
  265.7 0.4 multiply_reduce_fusion
  266.1 0.6 fusion.29
  266.8 0.6 dynamic-slice
  268.1 0.2 select_reduce_fusion
  268.3 71.6 %all-gather.6.cloned.1.call-done = bf16[2048,512]{1,0:T(8,128)(2,1)} async-done(((bf16[64,512]{1,0:T(8,128)(2,1)}), bf16[2048,512]{1,0:T(8,128)(2,1)}) %all-gather.6.cloned.1.call-update) | async-done | bytes 2097168 | tf_op jit(solution)/shard_map/all_gather | solution.py:101
  339.9 2.6 gather_fusion.3
  342.5 0.2 fusion.25
  342.7 0.2 dynamic-update-slice
  343.0 17.1 %all-reduce = f32[512]{0:T(512)S(1)} all-reduce(f32[512]{0:T(512)S(1)} %dynamic-update-slice), channel_id=2, replica_groups=mesh['expert'=32,'tensor'=8] {'tensor'}, use_global_device_ids=true, to_apply=%add | all-reduce | flops 512 | bytes 4096
  360.0 0.1 reshape.163
  360.1 0.7 fusion.27
  (50 shorter events, 0.6 us)
Async XLA Ops:
  7.2 147.8 %copy-start = (bf16[1,256,4096]{2,1,0:T(8,128)(2,1)S(1)}, bf16[1,256,4096]{2,1,0:T(8,128)(2,1)}, u32[]{:S(2)}) copy-start(bf16[1,256,4096]{2,1,0:T(8,128)(2,1)} %param.20) | copy-start | bytes 6291460
  7.2 4.1 %copy-start.6 = (s32[64,2]{0,1:T(2,128)S(1)}, s32[64,2]{0,1:T(2,128)}, u32[]{:S(2)}) copy-start(s32[64,2]{0,1:T(2,128)} %param.17) | copy-start | bytes 1540
  7.2 39.6 %reduce-scatter.3.cloned.1.call-start = ((), (), s32[]{:S(2)}) async-start(), calls=%async_computation.4 | async-start | bytes 589824 | tf_op jit(solution)/shard_map/reduce_scatter | solution.py:46
  11.2 2.3 copy-start.8
  11.2 35.6 %copy-start.2 = (bf16[64,512]{1,0:T(8,128)(2,1)S(1)}, bf16[64,512]{1,0:T(8,128)(2,1)}, u32[]{:S(2)}) copy-start(bf16[64,512]{1,0:T(8,128)(2,1)} %param.13) | copy-start | bytes 196612
  11.2 36.6 %copy-start.3 = (f32[512,8]{0,1:T(8,128)S(1)}, f32[512,8]{0,1:T(8,128)}, u32[]{:S(2)}) copy-start(f32[512,8]{0,1:T(8,128)} %param.16) | copy-start | bytes 49156
  11.2 36.6 %copy-start.4 = (f32[512]{0:T(512)S(1)}, f32[512]{0:T(512)}, u32[]{:S(2)}) copy-start(f32[512]{0:T(512)} %param.15) | copy-start | bytes 6148
  11.3 137.4 %all-gather.4.cloned.1.call-start = ((), (), s32[]{:S(2)}) async-start(), calls=%async_computation.5 | async-start | bytes 9437184 | tf_op jit(solution)/shard_map/all_gather | solution.py:82
  98.0 128.2 %reduce-scatter.5.cloned.1.call-start = ((), (), s32[]{:S(2)}) async-start(), calls=%async_computation.6 | async-start | bytes 9437184 | tf_op jit(solution)/shard_map/reduce_scatter | solution.py:14
  226.2 34.7 %all-to-all-start.1 = ((bf16[32,32,512]{2,1,0:T(8,128)(2,1)}), bf16[32,32,512]{2,1,0:T(8,128)(2,1)S(1)}, u32[]{:S(2)}, u32[]{:S(2)}) async-start(bf16[32,32,512]{2,1,0:T(8,128)(2,1)} %reduce-scatter.5.cloned.1.call-done), calls=%async_computation.3 | async-start | bytes 2097152 | tf_op jit(solution)/shard_map/all_to_all | solution.py:17
  235.8 104.1 %all-gather.6.cloned.1.call-start = ((), (), s32[]{:S(2)}) async-start(), calls=%async_computation.7 | async-start | bytes 2162688 | tf_op jit(solution)/shard_map/all_gather | solution.py:101
  263.6 3.2 copy-start.9
  263.6 4.5 %copy-start.5 = (s32[2048]{0:T(1024)S(1)}, s32[2048]{0:T(1024)}, u32[]{:S(2)}) copy-start(s32[2048]{0:T(1024)} %param.23) | copy-start | bytes 24580
  263.6 96.5 %copy-start.7 = (f32[512]{0:T(512)S(1)}, f32[512]{0:T(512)}, u32[]{:S(2)}) copy-start(f32[512]{0:T(512)} %param.22) | copy-start | bytes 6148
  342.7 18.2 %copy-start.1 = (bf16[64,512]{1,0:T(8,128)(2,1)}, bf16[64,512]{1,0:T(8,128)(2,1)S(1)}, u32[]{:S(2)}) copy-start(bf16[64,512]{1,0:T(8,128)(2,1)S(1)} %get-tuple-element.5) | copy-start | bytes 196612
Sparse Core Ops, SparseCore 0:
  11.4 35.4 reduce-scatter.2
  98.1 50.5 all-gather.3
  172.0 54.2 reduce-scatter.4
  266.9 72.9 all-gather.5
